TPU v7x, 32 devices: a whole 2x2x4 slice. The times are simulated.
32 devices in a mesh: ctx: 8 (over y, x, core), tp: 4 (over z).
Axes of the slice: x: 2, y: 2, z: 4, core: 2. Of those that a mesh axis runs over, the one named last changes fastest.
Arguments:
- qkv_input: bfloat16 [8192, 8192], P('ctx', 'tp'), may hold values from -48 to 48
- conv_weight: bfloat16 [4, 8192], P(None, 'tp'), may hold values from -3 to 3
- log_decay: float32 [32, 8192], P('tp', 'ctx'), may hold values from -1 to 0
- beta_gate: float32 [32, 8192], P('tp', 'ctx'), may hold values from 0.05 to 0.95
- output_gate: bfloat16 [8192, 4096], P('ctx', 'tp'), may hold values from -6 to 6
- norm_gain: float32 [128], replicated, may hold values from 0.25 to 1.75
- out_weight: bfloat16 [4096, 2048], P('tp'), may hold values from -0.09375 to 0.09375
Outputs:
- layer_out: bfloat16 [8192, 2048], P(('ctx', 'tp'))
All inputs are finite; a program needn't handle non-finite values.
Results may differ from a plain program's by a relative error of at most 0.015.
Values may be sent and summed in bfloat16 or wider, within the bound.
No kernel may reach another device: no remote copies, remote signals or barrier semaphores. Data moves between devices by JAX's collectives and lax.ppermute only.
A program may use at most 128 MiB of HBM per device.

v0:
```python
import jax
import jax.numpy as jnp
from jax import lax
from jax.sharding import PartitionSpec as P

VALUE_HEADS = 32
HK = 16
DK = 128
DV = 128
KCONV = 4
BLOCK = 64


exact_matmul_mode = lax.Precision.HIGHEST


def passed_along(block, axis, distance):
    devices = range(lax.axis_size(axis))
    route = [(i - distance, i) for i in devices if i - distance in devices]
    return lax.ppermute(block, axis, route)


def l2_rows(tensor):
    return tensor * lax.rsqrt(jnp.sum(tensor * tensor, axis=-1, keepdims=True) + 1e-06)


def matmul_heads(former, latter):
    return jnp.einsum("hij,hjk->hik", former, latter, precision=exact_matmul_mode)


def block_product(former, latter):
    return jnp.einsum("hnij,hnjk->hnik", former, latter, precision=exact_matmul_mode)


def unit_lower_inverse(system, identity_block):
    power = identity_block - system
    inverse = identity_block + power
    for squaring in range(5):
        power = block_product(power, power)
        inverse = inverse + block_product(inverse, power)
    return inverse


def body(qkv_input, conv_weight, log_decay, beta_gate, output_gate, norm_gain, out_weight):
    tokens = qkv_input.shape[0]
    head_ratio = VALUE_HEADS // HK
    group_width = 2 * DK + head_ratio * DV
    group_count = qkv_input.shape[1] // group_width
    head_count = group_count * head_ratio
    block_count = tokens // BLOCK
    last_rows = qkv_input[tokens - (KCONV - 1) :]
    prior_rows = passed_along(last_rows, "ctx", 1)
    padded = jnp.concatenate([prior_rows, qkv_input], 0).astype(jnp.float32)
    conv_taps = conv_weight.astype(jnp.float32)
    mixed = conv_taps[0] * padded[0:tokens]
    for offset in range(1, KCONV):
        mixed = mixed + conv_taps[offset] * padded[offset : offset + tokens]
    mixed = jax.nn.silu(mixed).reshape(tokens, group_count, group_width)
    queries = jnp.repeat(
        (l2_rows(mixed[:, :, :DK]) * DK ** (-0.5)).astype(jnp.bfloat16), head_ratio, axis=1
    )
    key_rows = jnp.repeat(
        l2_rows(mixed[:, :, DK : 2 * DK]).astype(jnp.bfloat16), head_ratio, axis=1
    )
    values = mixed[:, :, 2 * DK :].astype(jnp.bfloat16).reshape(tokens, head_count, DV)

    def blocked(tensor):
        return tensor.reshape(block_count, BLOCK, head_count, tensor.shape[-1]).transpose(
            2, 0, 1, 3
        )

    query_low = blocked(queries)
    key_low = blocked(key_rows)
    query_blocks = query_low.astype(jnp.float32)
    key_blocks = key_low.astype(jnp.float32)
    value_blocks = blocked(values).astype(jnp.float32)
    decay_blocks = log_decay.reshape(head_count, block_count, BLOCK)
    beta_blocks = beta_gate.reshape(head_count, block_count, BLOCK)
    position = jnp.arange(BLOCK)
    lower_mask = position[:, None] >= position[None, :]
    strict_mask = position[:, None] > position[None, :]
    identity_block = jnp.eye(BLOCK, dtype=jnp.float32)
    identity_key = jnp.eye(DK, dtype=jnp.float32)
    cumulative = jnp.cumsum(decay_blocks, axis=-1)
    exponent = jnp.where(lower_mask, cumulative[..., :, None] - cumulative[..., None, :], 0.0)
    damping = jnp.where(lower_mask, jnp.exp(exponent), 0.0)
    key_gram = jnp.einsum("hnik,hnjk->hnij", key_low, key_low, preferred_element_type=jnp.float32)
    system = identity_block + jnp.where(
        strict_mask, beta_blocks[..., :, None] * key_gram * damping, 0.0
    )
    inverse_system = unit_lower_inverse(system, identity_block)
    right_sides = jnp.concatenate(
        [
            beta_blocks[..., None] * value_blocks,
            (beta_blocks * jnp.exp(cumulative))[..., None] * key_blocks,
        ],
        -1,
    )
    solved = block_product(inverse_system, right_sides)
    fresh_values = solved[..., :DV]
    wy_weights = solved[..., DV:]
    scores = (
        jnp.einsum("hnik,hnjk->hnij", query_low, key_low, preferred_element_type=jnp.float32)
        * damping
    )
    query_decayed = jnp.exp(cumulative)[..., None] * query_blocks
    last_cum = cumulative[..., -1]
    key_decayed = jnp.exp(last_cum[..., None] - cumulative)[..., None] * key_blocks
    last_gain = jnp.exp(last_cum)
    block_trans = last_gain[..., None, None] * identity_key - jnp.einsum(
        "hnik,hnij->hnkj", key_decayed, wy_weights, precision=exact_matmul_mode
    )
    block_state = jnp.einsum(
        "hnik,hniv->hnkv", key_decayed, fresh_values, precision=exact_matmul_mode
    )

    def by_block(tensor):
        return jnp.moveaxis(tensor, 1, 0)

    block_items = (
        by_block(query_decayed),
        by_block(wy_weights),
        by_block(fresh_values),
        by_block(scores),
        by_block(key_decayed),
        by_block(last_gain),
    )
    zero_state = jnp.zeros((head_count, DK, DV), jnp.float32)
    unit_trans = jnp.broadcast_to(identity_key, (head_count, DK, DK))

    def emit_pieces(present_state, query_decay_rows, householder_block, fresh_block, score_block):
        updated_value_rows = fresh_block - jnp.einsum(
            "efm,emj->efj", householder_block, present_state, precision=exact_matmul_mode
        )
        emitted_output = jnp.einsum(
            "efm,emj->efj", query_decay_rows, present_state, precision=exact_matmul_mode
        )
        emitted_output = emitted_output + jnp.einsum(
            "hcj,hjv->hcv", score_block, updated_value_rows, precision=exact_matmul_mode
        )
        return (updated_value_rows, emitted_output)

    def advance(present_state, gain_block, key_decay_rows, updated_value_rows):
        return gain_block[:, None, None] * present_state + jnp.einsum(
            "qpi,qpj->qij", key_decay_rows, updated_value_rows, precision=exact_matmul_mode
        )

    def fold_blocks(carry_pair, block_item):
        acc_trans, acc_state = carry_pair
        trans_block, state_block = block_item
        return (
            (
                matmul_heads(trans_block, acc_trans),
                matmul_heads(trans_block, acc_state) + state_block,
            ),
            None,
        )

    (dev_trans, dev_state), _ = lax.scan(
        fold_blocks, (unit_trans, zero_state), (by_block(block_trans), by_block(block_state))
    )

    def relay(turn_index, present_state):
        leaving = matmul_heads(dev_trans, present_state) + dev_state
        return passed_along(leaving.astype(jnp.bfloat16), "ctx", 1).astype(leaving.dtype)

    entering = lax.fori_loop(0, lax.axis_size("ctx") - 1, relay, zero_state)

    def emit_block(present_state, block_item):
        (
            query_decay_rows,
            householder_block,
            fresh_block,
            score_block,
            key_decay_rows,
            gain_block,
        ) = block_item
        updated_value_rows, emitted_output = emit_pieces(
            present_state, query_decay_rows, householder_block, fresh_block, score_block
        )
        return (
            advance(present_state, gain_block, key_decay_rows, updated_value_rows),
            emitted_output,
        )

    _, outputs = lax.scan(emit_block, entering, block_items)
    attended = outputs.transpose(0, 2, 1, 3).reshape(tokens, head_count, DV)
    gate_values = jax.nn.silu(output_gate.astype(jnp.float32)).reshape(tokens, head_count, DV)
    scaled = attended * lax.rsqrt(jnp.mean(attended * attended, axis=-1, keepdims=True) + 1e-06)
    normed = (
        (scaled * norm_gain * gate_values).astype(jnp.bfloat16).reshape(tokens, head_count * DV)
    )
    return lax.psum_scatter(
        jnp.dot(normed, out_weight, preferred_element_type=jnp.float32).astype(jnp.bfloat16),
        "tp",
        scatter_dimension=0,
        tiled=True,
    )


def solution(mesh):
    in_specs = (
        P("ctx", "tp"),
        P(None, "tp"),
        P("tp", "ctx"),
        P("tp", "ctx"),
        P("ctx", "tp"),
        P(),
        P("tp", None),
    )
    out_specs = P(("ctx", "tp"), None)
    return jax.shard_map(body, mesh=mesh, in_specs=in_specs, out_specs=out_specs, check_vma=False)
```

profile of v0, /device:TPU:0, one launch (start us, length us, event | category | flops | bytes accessed | tf_op | source)
XLA Modules:
  0.0 531.3 jit_solution(7475242843117291683)
XLA Ops:
  7.3 2.4 collective-permute-start.1
  14.6 3.4 maximum_convert_fusion
  18.0 6.5 %divide_multiply_fusion = f32[1024,2048]{1,0:T(8,128)} fusion(f32[1027,2048]{1,0:T(8,128)S(1)} %maximum_convert_fusion, f32[2048]{0:T(1024)S(1)} %bitcast.173, f32[2048]{0:T(1024)S(1)} %bitcast.172, f32[2048]{0:T(1024)S(1)} %bitcast.171, f32[2048]{0:T(1024)S(1)} %bitcast.170), kind=kLoop, calls=%fused_computation.50 | loop fusion | flops 23068672 | bytes 41975808 | tf_op jit(solution)/shard_map/jit(silu)/mul | solution.py:58
  24.5 10.8 %reshape.88 = f32[1024,4,512]{2,1,0:T(4,128)} reshape(f32[1024,2048]{1,0:T(8,128)} %divide_multiply_fusion) | data formatting | bytes 16777216 | tf_op jit(solution)/shard_map/reshape | solution.py:58
  35.4 4.5 multiply_reduce_fusion.1
  40.0 6.9 %multiply_convert_fusion = (bf16[1024,4,128]{2,1,0:T(4,128)(2,1)}, bf16[1024,4,128]{2,1,0:T(4,128)(2,1)S(1)}) fusion(f32[1024,4,512]{2,1,0:T(4,128)} %reshape.88, f32[1024,4]{1,0:T(8,128)S(1)} %get-tuple-element.245, f32[1024,4]{1,0:T(8,128)S(1)} %get-tuple-element.246), kind=kLoop, calls=%fused_computation.88 | loop fusion | flops 2621440 | bytes 6324224 | tf_op jit(solution)/shard_map/convert_element_type | solution.py:60
  47.4 2.3 add_subtract_fusion
  49.7 5.2 fusion.72
  54.9 6.1 %add_add_fusion = f32[8,16,64,64]{3,2,1,0:T(8,128)S(1)} fusion(f32[8,16,64,64]{3,2,1,0:T(8,128)S(1)} %add_subtract_fusion, f32[8,16,64,64]{3,2,1,0:T(8,128)S(1)} %fusion.72, f32[64,64]{1,0:T(8,128)S(1)} %fusion.68), kind=kOutput, calls=%fused_computation.77 | convolution fusion | flops 404226048 | bytes 6307840 | tf_op jit(solution)/shard_map/hnij,hnjk->hnik/dot_general | solution.py:32
  61.0 4.8 fusion.73
  65.8 4.8 fusion.61
  70.7 5.2 fusion.74
  75.9 5.7 %convolution_add_fusion.5 = f32[8,16,64,64]{3,2,1,0:T(8,128)S(1)} fusion(f32[8,16,64,64]{3,2,1,0:T(8,128)S(1)} %add_add_fusion, f32[8,16,64,64]{3,2,1,0:T(8,128)S(1)} %fusion.73), kind=kOutput, calls=%fused_computation.84 | convolution fusion | flops 403177472 | bytes 6291456 | tf_op jit(solution)/shard_map/hnij,hnjk->hnik/dot_general | solution.py:32
  81.6 5.3 %fusion.76 = f32[8,16,64,64]{3,2,1,0:T(8,128)S(1)} fusion(f32[8,16,64,64]{3,2,1,0:T(8,128)S(1)} %fusion.74), kind=kOutput, calls=%fused_computation.118 | convolution fusion | flops 402653184 | bytes 4194304 | tf_op jit(solution)/shard_map/hnij,hnjk->hnik/dot_general | solution.py:32
  86.9 5.8 %fusion.75 = f32[8,16,64,64]{3,2,1,0:T(8,128)S(1)} fusion(f32[8,16,64,64]{3,2,1,0:T(8,128)S(1)} %convolution_add_fusion.5, f32[8,16,64,64]{3,2,1,0:T(8,128)S(1)} %fusion.74), kind=kOutput, calls=%fused_computation.117 | convolution fusion | flops 402653184 | bytes 6291456 | tf_op jit(solution)/shard_map/hnij,hnjk->hnik/dot_general | solution.py:32
  92.7 5.9 %fusion.77 = f32[8,16,64,64]{3,2,1,0:T(8,128)} fusion(f32[8,16,64,64]{3,2,1,0:T(8,128)S(1)} %fusion.76), kind=kOutput, calls=%fused_computation.119 | convolution fusion | flops 402653184 | bytes 4194304 | tf_op jit(solution)/shard_map/hnij,hnjk->hnik/dot_general | solution.py:32
  98.7 6.1 %convolution_add_fusion.4 = f32[8,16,64,64]{3,2,1,0:T(8,128)} fusion(f32[8,16,64,64]{3,2,1,0:T(8,128)S(1)} %fusion.76, f32[8,16,64,64]{3,2,1,0:T(8,128)S(1)} %convolution_add_fusion.5, f32[8,16,64,64]{3,2,1,0:T(8,128)S(1)} %fusion.75), kind=kOutput, calls=%fused_computation.82 | convolution fusion | flops 403701760 | bytes 8388608 | tf_op jit(solution)/shard_map/hnij,hnjk->hnik/dot_general | solution.py:32
  104.8 2.6 convert_multiply_fusion.1
  107.4 5.5 %reshape.90 = f32[16,64,8,128]{3,2,1,0:T(8,128)} reshape(f32[1024,4,256]{2,1,0:T(4,128)} %fusion.61) | data formatting | bytes 8388608 | tf_op jit(solution)/shard_map/convert_element_type | solution.py:76
  112.9 4.8 bitcast_multiply_fusion.4
  119.1 5.9 %fusion.78 = f32[8,16,64,64]{3,2,1,0:T(8,128)} fusion(f32[8,16,64,64]{3,2,1,0:T(8,128)S(1)} %copy-done.5, f32[8,16,64,64]{3,2,1,0:T(8,128)S(1)} %copy-done.6), kind=kOutput, calls=%fused_computation.120 | convolution fusion | flops 402653184 | bytes 6291456 | tf_op jit(solution)/shard_map/hnij,hnjk->hnik/dot_general | solution.py:32
  125.0 12.3 %fusion.35 = f32[8,16,64,256]{3,2,1,0:T(8,128)S(1)} fusion(f32[8,16,64,128]{3,2,1,0:T(8,128)} %convert_multiply_fusion.1, f32[8,16,64,128]{3,2,1,0:T(8,128)} %bitcast_multiply_fusion.4, f32[8,16,64,64]{3,2,1,0:T(8,128)} %convolution_add_fusion.4, f32[8,16,64,64]{3,2,1,0:T(8,128)} %fusion.78), kind=kOutput, calls=%fused_computation.45 | convolution fusion | flops 1613234176 | bytes 20971520 | tf_op jit(solution)/shard_map/hnij,hnjk->hnik/dot_general | solution.py:32
  137.3 4.4 slice_bitcast_fusion.1
  141.8 16.7 %fusion.56 = f32[16,8,128,128]{3,2,0,1:T(8,128)} fusion(f32[8,16,64,256]{3,2,1,0:T(8,128)S(1)} %fusion.35, bf16[8,16,64,128]{3,2,1,0:T(8,128)(2,1)S(1)} %bitcast.158, f32[8,16,64]{2,1,0:T(8,128)S(1)} %get-tuple-element.239), kind=kOutput, calls=%fused_computation.81 | convolution fusion | flops 1612709888 | bytes 14745600 | tf_op jit(solution)/shard_map/hnik,hniv->hnkv/dot_general | solution.py:113
  158.5 17.9 %bitcast_subtract_fusion = f32[16,8,128,128]{3,2,0,1:T(8,128)} fusion(f32[128,128]{1,0:T(8,128)S(1)} %fusion.67, f32[16,8]{0,1:T(8,128)S(1)} %exponential_bitcast_fusion, f32[8,16,64,256]{3,2,1,0:T(8,128)S(1)} %fusion.35, bf16[8,16,64,128]{3,2,1,0:T(8,128)(2,1)S(1)} %bitcast.159, f32[8,16,64]{2,1,0:T(8,128)S(1)} %get-tuple-element.239), kind=kOutput, calls=%fused_computation.49 | convolution fusion | flops 1616904192 | bytes 14815232 | tf_op jit(solution)/shard_map/hnik,hnij->hnkj/dot_general | solution.py:110
  176.4 59.1 %while.37 = (s32[]{:T(128)}, f32[8,128,128]{2,1,0:T(8,128)S(1)}, f32[8,128,128]{2,1,0:T(8,128)S(1)}, f32[16,8,128,128]{3,2,0,1:T(8,128)}, f32[16,8,128,128]{3,2,0,1:T(8,128)}, /*index=5*/s32[]{:T(128)}, s32[]{:T(128)}) while((s32[]{:T(128)}, f32[8,128,128]{2,1,0:T(8,128)S(1)}, f32[8,128,128]{2,1,0:T(8,128)S(1)}, ...), condition=%wide.region_3.4_spmd.clone, body=%wide.region_2.3_spmd.clone.sunk | while | flops 402915328 | bytes 5768791 | solution.py:159
  237.2 2.7 bitcast_multiply_fusion.1
  239.9 2.6 bitcast_multiply_fusion.2
  242.5 2.5 bitcast_multiply_fusion.3
  245.0 54.5 %while.38 = (s32[]{:T(128)}, f32[8,128,128]{2,1,0:T(8,128)S(1)}, f32[8,128,128]{2,1,0:T(8,128)S(1)}, f32[8,128,128]{2,1,0:T(8,128)S(1)}, s32[]{:T(128)}, /*index=5*/s32[]{:T(128)}) while((s32[]{:T(128)}, f32[8,128,128]{2,1,0:T(8,128)S(1)}, f32[8,128,128]{2,1,0:T(8,128)S(1)}, f32[8,128,128]{2,1,0:T(8,128)S(1)}, s32[]{:T(128)}, ...), condition=%wide.region_5.6_spmd.clone, body=%wide.region_4.5_spmd.clone.sunk | while | flops 201850880 | bytes 3670135 | solution.py:167
  245.9 4.5 collective-permute-start
  252.3 4.1 collective-permute-start
  258.2 6.6 %collective-permute-start = (bf16[8,128,128]{2,1,0:T(8,128)(2,1)S(1)}, bf16[8,128,128]{2,1,0:T(8,128)(2,1)S(1)}, u32[]{:S(2)}, u32[]{:S(2)}) collective-permute-start(bf16[8,128,128]{2,1,0:T(8,128)(2,1)S(1)} %fusion.145), channel_id=1, source_target_pairs={{0,4},{4,8},{8,12},{12,16},{16,20},{20,24},{24,28},{1,5},{5,9},{9,... | collective-permute-start | bytes 786440 | tf_op jit(solution)/shard_map/while/body/eval_jaxpr/ppermute | solution.py:20
  266.6 6.6 %collective-permute-start = (bf16[8,128,128]{2,1,0:T(8,128)(2,1)S(1)}, bf16[8,128,128]{2,1,0:T(8,128)(2,1)S(1)}, u32[]{:S(2)}, u32[]{:S(2)}) collective-permute-start(bf16[8,128,128]{2,1,0:T(8,128)(2,1)S(1)} %fusion.145), channel_id=1, source_target_pairs={{0,4},{4,8},{8,12},{12,16},{16,20},{20,24},{24,28},{1,5},{5,9},{9,... | collective-permute-start | bytes 786440 | tf_op jit(solution)/shard_map/while/body/eval_jaxpr/ppermute | solution.py:20
  275.0 6.6 %collective-permute-start = (bf16[8,128,128]{2,1,0:T(8,128)(2,1)S(1)}, bf16[8,128,128]{2,1,0:T(8,128)(2,1)S(1)}, u32[]{:S(2)}, u32[]{:S(2)}) collective-permute-start(bf16[8,128,128]{2,1,0:T(8,128)(2,1)S(1)} %fusion.145), channel_id=1, source_target_pairs={{0,4},{4,8},{8,12},{12,16},{16,20},{20,24},{24,28},{1,5},{5,9},{9,... | collective-permute-start | bytes 786440 | tf_op jit(solution)/shard_map/while/body/eval_jaxpr/ppermute | solution.py:20
  283.4 6.6 %collective-permute-start = (bf16[8,128,128]{2,1,0:T(8,128)(2,1)S(1)}, bf16[8,128,128]{2,1,0:T(8,128)(2,1)S(1)}, u32[]{:S(2)}, u32[]{:S(2)}) collective-permute-start(bf16[8,128,128]{2,1,0:T(8,128)(2,1)S(1)} %fusion.145), channel_id=1, source_target_pairs={{0,4},{4,8},{8,12},{12,16},{16,20},{20,24},{24,28},{1,5},{5,9},{9,... | collective-permute-start | bytes 786440 | tf_op jit(solution)/shard_map/while/body/eval_jaxpr/ppermute | solution.py:20
  291.8 6.6 %collective-permute-start = (bf16[8,128,128]{2,1,0:T(8,128)(2,1)S(1)}, bf16[8,128,128]{2,1,0:T(8,128)(2,1)S(1)}, u32[]{:S(2)}, u32[]{:S(2)}) collective-permute-start(bf16[8,128,128]{2,1,0:T(8,128)(2,1)S(1)} %fusion.145), channel_id=1, source_target_pairs={{0,4},{4,8},{8,12},{12,16},{16,20},{20,24},{24,28},{1,5},{5,9},{9,... | collective-permute-start | bytes 786440 | tf_op jit(solution)/shard_map/while/body/eval_jaxpr/ppermute | solution.py:20
  299.6 117.1 %while.36 = (s32[]{:T(128)}, f32[8,128,128]{2,1,0:T(8,128)S(1)}, f32[16,8,64,128]{3,2,1,0:T(8,128)}, f32[16,8]{1,0:T(8,128)S(1)}, f32[16,8,64,128]{3,2,0,1:T(8,1...) while((s32[]{:T(128)}, f32[8,128,128]{2,1,0:T(8,128)S(1)}, ...), condition=%wide.region_8.9_spmd, body=%wide.region_7.8_spmd.sunk | while | flops 352714752 | bytes 4984009 | solution.py:186
  304.8 2.0 convolution_add_fusion.8
  310.1 2.1 fusion.137
  312.2 2.0 convolution_add_fusion.8
  317.4 2.0 fusion.137
  319.5 2.0 convolution_add_fusion.8
  326.8 2.0 convolution_add_fusion.8
  332.1 2.1 fusion.137
  334.1 2.0 convolution_add_fusion.8
  341.5 2.0 convolution_add_fusion.8
  348.8 2.0 convolution_add_fusion.8
  356.1 2.0 convolution_add_fusion.8
  361.4 2.1 fusion.137
  363.4 2.0 convolution_add_fusion.8
  370.7 2.0 convolution_add_fusion.8
  376.0 2.0 fusion.137
  378.1 2.0 convolution_add_fusion.8
  383.3 2.1 fusion.137
  385.4 2.0 convolution_add_fusion.8
  390.6 2.1 fusion.137
  392.7 2.0 convolution_add_fusion.8
  398.0 2.0 fusion.137
  400.0 2.0 convolution_add_fusion.8
  416.7 3.3 multiply_reduce_fusion
  420.3 5.6 %copy.53 = f32[16,64,8,128]{3,2,1,0:T(8,128)S(1)} copy(f32[16,64,8,128]{3,1,2,0:T(8,128)} %bitcast.162) | data formatting | bytes 8388608 | tf_op jit(solution)/shard_map/transpose | solution.py:187
  428.1 6.8 %convolution_convert_fusion = bf16[1024,2048]{1,0:T(8,128)(2,1)} fusion(bf16[1024,2048]{1,0:T(8,128)(2,1)S(1)} %copy-done.8, bf16[1024,1024]{1,0:T(8,128)(2,1)S(1)} %copy-done.9, f32[128,8,8,128]{3,2,1,0:T(8,128)S(1)} %bitcast.165, f32[128,8,8,128]{3,2,1,0:T(8,128)S(1)} %bitcast.166, f32[1024]{0:T(1024)S(1)} %broadcast_bitcast_fusion), kind=kOutput, calls=%fused_computation.80 | convolution fusion | flops 4306501632 | bytes 18878464 | tf_op jit(solution)/shard_map/dot_general | solution.py:194
  434.9 89.0 %reduce-scatter.2.cloned.1.call-done = bf16[256,2048]{1,0:T(8,128)(2,1)} async-done(((bf16[1024,2048]{1,0:T(8,128)(2,1)}), bf16[256,2048]{1,0:T(8,128)(2,1)}) %reduce-scatter.2.cloned.1.call-update) | async-done | bytes 1048592 | tf_op jit(solution)/shard_map/reduce_scatter | solution.py:193
  (192 shorter events, 154.0 us)
Async XLA Ops:
  6.5 7.9 %copy-start = (f32[128]{0:T(128)S(1)}, f32[128]{0:T(128)}, u32[]{:S(2)}) copy-start(f32[128]{0:T(128)} %param.18) | copy-start | bytes 1540
  6.5 517.4 %reduce-scatter.2.cloned.1.call-start = ((), (), s32[]{:S(2)}) async-start(), calls=%async_computation.1 | async-start | bytes 5242880 | tf_op jit(solution)/shard_map/reduce_scatter | solution.py:193
  7.3 7.3 %collective-permute-start.1 = (bf16[3,2048]{1,0:T(4,128)(2,1)S(1)}, bf16[3,2048]{1,0:T(4,128)(2,1)S(1)}, u32[]{:S(2)}, u32[]{:S(2)}) collective-permute-start(bf16[3,2048]{1,0:T(4,128)(2,1)S(1)} %slice.48), channel_id=1, source_target_pairs={{0,4},{4,8},{8,12},{12,16},{16,20},{20,24},{24,28},{1,5},{5,9},{9,... | collective-permute-start | bytes 36872 | tf_op jit(solution)/shard_map/ppermute | solution.py:20
  47.4 57.4 %copy-start.2 = (bf16[1024,4,2,128]{3,0,2,1:T(8,128)(2,1)}, bf16[1024,4,2,128]{3,0,2,1:T(8,128)(2,1)S(1)}, u32[]{:S(2)}) copy-start(bf16[1024,4,2,128]{3,0,2,1:T(8,128)(2,1)S(1)} %broadcast_in_dim.62) | copy-start | bytes 6291460
  112.9 4.8 copy-start.5
  112.9 6.2 %copy-start.6 = (f32[8,16,64,64]{3,2,1,0:T(8,128)S(1)}, f32[8,16,64,64]{3,2,1,0:T(8,128)}, u32[]{:S(2)}) copy-start(f32[8,16,64,64]{3,2,1,0:T(8,128)} %fusion.77) | copy-start | bytes 6291460
  137.3 4.5 copy-start.3
  176.4 59.2 %copy-start.7 = (bf16[1024,4,128]{2,1,0:T(4,128)(2,1)S(1)}, bf16[1024,4,128]{2,1,0:T(4,128)(2,1)}, u32[]{:S(2)}) copy-start(bf16[1024,4,128]{2,1,0:T(4,128)(2,1)} %get-tuple-element.233) | copy-start | bytes 3145732
  235.6 1.6 copy-start.4
  245.9 5.7 %collective-permute-start = (bf16[8,128,128]{2,1,0:T(8,128)(2,1)S(1)}, bf16[8,128,128]{2,1,0:T(8,128)(2,1)S(1)}, u32[]{:S(2)}, u32[]{:S(2)}) collective-permute-start(bf16[8,128,128]{2,1,0:T(8,128)(2,1)S(1)} %fusion.145), channel_id=1, source_target_pairs={{0,4},{4,8},{8,12},{12,16},{16,20},{20,24},{24,28},{1,5},{5,9},{9,... | collective-permute-start | bytes 786440 | tf_op jit(solution)/shard_map/while/body/eval_jaxpr/ppermute | solution.py:20
  252.3 5.2 collective-permute-start
  258.2 7.7 %collective-permute-start = (bf16[8,128,128]{2,1,0:T(8,128)(2,1)S(1)}, bf16[8,128,128]{2,1,0:T(8,128)(2,1)S(1)}, u32[]{:S(2)}, u32[]{:S(2)}) collective-permute-start(bf16[8,128,128]{2,1,0:T(8,128)(2,1)S(1)} %fusion.145), channel_id=1, source_target_pairs={{0,4},{4,8},{8,12},{12,16},{16,20},{20,24},{24,28},{1,5},{5,9},{9,... | collective-permute-start | bytes 786440 | tf_op jit(solution)/shard_map/while/body/eval_jaxpr/ppermute | solution.py:20
  266.6 7.7 %collective-permute-start = (bf16[8,128,128]{2,1,0:T(8,128)(2,1)S(1)}, bf16[8,128,128]{2,1,0:T(8,128)(2,1)S(1)}, u32[]{:S(2)}, u32[]{:S(2)}) collective-permute-start(bf16[8,128,128]{2,1,0:T(8,128)(2,1)S(1)} %fusion.145), channel_id=1, source_target_pairs={{0,4},{4,8},{8,12},{12,16},{16,20},{20,24},{24,28},{1,5},{5,9},{9,... | collective-permute-start | bytes 786440 | tf_op jit(solution)/shard_map/while/body/eval_jaxpr/ppermute | solution.py:20
  275.0 7.7 %collective-permute-start = (bf16[8,128,128]{2,1,0:T(8,128)(2,1)S(1)}, bf16[8,128,128]{2,1,0:T(8,128)(2,1)S(1)}, u32[]{:S(2)}, u32[]{:S(2)}) collective-permute-start(bf16[8,128,128]{2,1,0:T(8,128)(2,1)S(1)} %fusion.145), channel_id=1, source_target_pairs={{0,4},{4,8},{8,12},{12,16},{16,20},{20,24},{24,28},{1,5},{5,9},{9,... | collective-permute-start | bytes 786440 | tf_op jit(solution)/shard_map/while/body/eval_jaxpr/ppermute | solution.py:20
  283.4 7.7 %collective-permute-start = (bf16[8,128,128]{2,1,0:T(8,128)(2,1)S(1)}, bf16[8,128,128]{2,1,0:T(8,128)(2,1)S(1)}, u32[]{:S(2)}, u32[]{:S(2)}) collective-permute-start(bf16[8,128,128]{2,1,0:T(8,128)(2,1)S(1)} %fusion.145), channel_id=1, source_target_pairs={{0,4},{4,8},{8,12},{12,16},{16,20},{20,24},{24,28},{1,5},{5,9},{9,... | collective-permute-start | bytes 786440 | tf_op jit(solution)/shard_map/while/body/eval_jaxpr/ppermute | solution.py:20
  291.8 7.7 %collective-permute-start = (bf16[8,128,128]{2,1,0:T(8,128)(2,1)S(1)}, bf16[8,128,128]{2,1,0:T(8,128)(2,1)S(1)}, u32[]{:S(2)}, u32[]{:S(2)}) collective-permute-start(bf16[8,128,128]{2,1,0:T(8,128)(2,1)S(1)} %fusion.145), channel_id=1, source_target_pairs={{0,4},{4,8},{8,12},{12,16},{16,20},{20,24},{24,28},{1,5},{5,9},{9,... | collective-permute-start | bytes 786440 | tf_op jit(solution)/shard_map/while/body/eval_jaxpr/ppermute | solution.py:20
  420.3 6.8 %copy-start.9 = (bf16[1024,1024]{1,0:T(8,128)(2,1)S(1)}, bf16[1024,1024]{1,0:T(8,128)(2,1)}, u32[]{:S(2)}) copy-start(bf16[1024,1024]{1,0:T(8,128)(2,1)} %param.17) | copy-start | bytes 6291460
  425.9 2.2 copy-start.8
  428.1 95.9 %copy-start.1 = (f32[128]{0:T(128)S(1)}, f32[128]{0:T(128)}, u32[]{:S(2)}) copy-start(f32[128]{0:T(128)} %param.18) | copy-start | bytes 1540
Sparse Core Ops, SparseCore 0:
  435.1 88.8 reduce-scatter.1
where the time goes:
time: 540 us; the launch traced here: 531 us
  matrix products  293 us (54%)
  waiting for transfers between devices  97 us (18%)
  other arithmetic  44.5 us (8%)
  starting transfers between devices  43.7 us (8%)
  local copies, waits for them, and re-layouts  37.1 us (7%)
  between operations  14.2 us (3%)
    reduce_scatter x1, waiting for transfers between devices, body(): lax.psum_scatter(jnp.dot(normed, out_weight, preferred_element_type=jnp.f...  89 us
    dot_general x11, matrix products, block_product(): jnp.einsum('hnij,hnjk->hnik', former, latter, precision=exact_matmul_mode)  68.4 us
    dot_general x39, matrix products, matmul_heads(): jnp.einsum('hij,hjk->hik', former, latter, precision=exact_matmul_mode)  61.7 us
    ppermute x8, starting transfers between devices, passed_along(): return lax.ppermute(block, axis, route)  43.7 us
    dot_general x16, matrix products, emit_pieces(): jnp.einsum('hcj,hjv->hcv', score_block, updated_value_rows, precision=exa...  32.8 us
    dot_general x16, matrix products, advance(): jnp.einsum('qpi,qpj->qij', key_decay_rows, updated_value_rows, precision=...  32.8 us
    dot_general x16, matrix products, emit_pieces(): jnp.einsum('efm,emj->efj', householder_block, present_state, precision=ex...  26.1 us
    dot_general x16, matrix products, emit_pieces(): jnp.einsum('efm,emj->efj', query_decay_rows, present_state, precision=exa...  24.8 us
  transfers between devices with their start and end apart: 9, of which 8 were waited for; matrix products, arithmetic and copies ran while one was open for 1% of the time, Pallas kernels for 0%

commit v1 on v0

--- a/solution.py
+++ b/solution.py
@@ -114,88 +114,87 @@
         "hnik,hniv->hnkv", key_decayed, fresh_values, precision=exact_matmul_mode
     )
 
-    def by_block(tensor):
-        return jnp.moveaxis(tensor, 1, 0)
-
-    block_items = (
-        by_block(query_decayed),
-        by_block(wy_weights),
-        by_block(fresh_values),
-        by_block(scores),
-        by_block(key_decayed),
-        by_block(last_gain),
-    )
+    lanes = lax.axis_size("tp")
+    steps = block_count // lanes
+
+    def compose(first, second):
+        first_trans, first_state = first
+        second_trans, second_state = second
+        return (
+            block_product(second_trans, first_trans),
+            block_product(second_trans, first_state) + second_state,
+        )
+
+    level = (block_trans, block_state)
+    while level[0].shape[1] > lanes:
+        level = compose(
+            (level[0][:, 0::2], level[1][:, 0::2]), (level[0][:, 1::2], level[1][:, 1::2])
+        )
+    lane_trans, lane_state = level
+    while level[0].shape[1] > 1:
+        level = compose(
+            (level[0][:, 0::2], level[1][:, 0::2]), (level[0][:, 1::2], level[1][:, 1::2])
+        )
+    dev_trans, dev_state = level[0][:, 0], level[1][:, 0]
     zero_state = jnp.zeros((head_count, DK, DV), jnp.float32)
-    unit_trans = jnp.broadcast_to(identity_key, (head_count, DK, DK))
-
-    def emit_pieces(present_state, query_decay_rows, householder_block, fresh_block, score_block):
-        updated_value_rows = fresh_block - jnp.einsum(
-            "efm,emj->efj", householder_block, present_state, precision=exact_matmul_mode
-        )
-        emitted_output = jnp.einsum(
-            "efm,emj->efj", query_decay_rows, present_state, precision=exact_matmul_mode
-        )
-        emitted_output = emitted_output + jnp.einsum(
-            "hcj,hjv->hcv", score_block, updated_value_rows, precision=exact_matmul_mode
-        )
-        return (updated_value_rows, emitted_output)
-
-    def advance(present_state, gain_block, key_decay_rows, updated_value_rows):
-        return gain_block[:, None, None] * present_state + jnp.einsum(
-            "qpi,qpj->qij", key_decay_rows, updated_value_rows, precision=exact_matmul_mode
-        )
-
-    def fold_blocks(carry_pair, block_item):
-        acc_trans, acc_state = carry_pair
-        trans_block, state_block = block_item
-        return (
-            (
-                matmul_heads(trans_block, acc_trans),
-                matmul_heads(trans_block, acc_state) + state_block,
-            ),
-            None,
-        )
-
-    (dev_trans, dev_state), _ = lax.scan(
-        fold_blocks, (unit_trans, zero_state), (by_block(block_trans), by_block(block_state))
-    )
 
     def relay(turn_index, present_state):
         leaving = matmul_heads(dev_trans, present_state) + dev_state
         return passed_along(leaving.astype(jnp.bfloat16), "ctx", 1).astype(leaving.dtype)
 
     entering = lax.fori_loop(0, lax.axis_size("ctx") - 1, relay, zero_state)
-
-    def emit_block(present_state, block_item):
-        (
-            query_decay_rows,
-            householder_block,
-            fresh_block,
-            score_block,
-            key_decay_rows,
-            gain_block,
-        ) = block_item
-        updated_value_rows, emitted_output = emit_pieces(
-            present_state, query_decay_rows, householder_block, fresh_block, score_block
-        )
-        return (
-            advance(present_state, gain_block, key_decay_rows, updated_value_rows),
-            emitted_output,
-        )
-
-    _, outputs = lax.scan(emit_block, entering, block_items)
-    attended = outputs.transpose(0, 2, 1, 3).reshape(tokens, head_count, DV)
-    gate_values = jax.nn.silu(output_gate.astype(jnp.float32)).reshape(tokens, head_count, DV)
-    scaled = attended * lax.rsqrt(jnp.mean(attended * attended, axis=-1, keepdims=True) + 1e-06)
-    normed = (
-        (scaled * norm_gain * gate_values).astype(jnp.bfloat16).reshape(tokens, head_count * DV)
-    )
-    return lax.psum_scatter(
-        jnp.dot(normed, out_weight, preferred_element_type=jnp.float32).astype(jnp.bfloat16),
-        "tp",
-        scatter_dimension=0,
-        tiled=True,
-    )
+    lane_entry = [entering]
+    for lane in range(1, lanes):
+        lane_entry.append(
+            matmul_heads(lane_trans[:, lane - 1], lane_entry[-1]) + lane_state[:, lane - 1]
+        )
+    present_state = jnp.stack(lane_entry, 1)
+
+    def by_step(tensor):
+        return tensor.reshape((head_count, lanes, steps) + tensor.shape[2:])
+
+    query_decayed = by_step(query_decayed)
+    wy_weights = by_step(wy_weights)
+    fresh_values = by_step(fresh_values)
+    scores = by_step(scores)
+    key_decayed = by_step(key_decayed)
+    last_gain = by_step(last_gain)
+    gate_values = jax.nn.silu(output_gate.astype(jnp.float32)).reshape(
+        lanes, steps, BLOCK, head_count, DV
+    )
+    pieces = []
+    for step in range(steps):
+        updated_value_rows = fresh_values[:, :, step] - block_product(
+            wy_weights[:, :, step], present_state
+        )
+        emitted = block_product(query_decayed[:, :, step], present_state) + block_product(
+            scores[:, :, step], updated_value_rows
+        )
+        if step + 1 < steps:
+            present_state = last_gain[:, :, step][..., None, None] * present_state + jnp.einsum(
+                "hnpi,hnpj->hnij",
+                key_decayed[:, :, step],
+                updated_value_rows,
+                precision=exact_matmul_mode,
+            )
+        attended = emitted.transpose(1, 2, 0, 3)
+        scaled = attended * lax.rsqrt(jnp.mean(attended * attended, axis=-1, keepdims=True) + 1e-06)
+        normed = (
+            (scaled * norm_gain * gate_values[:, step])
+            .astype(jnp.bfloat16)
+            .reshape(lanes * BLOCK, head_count * DV)
+        )
+        pieces.append(
+            lax.psum_scatter(
+                jnp.dot(normed, out_weight, preferred_element_type=jnp.float32).astype(
+                    jnp.bfloat16
+                ),
+                "tp",
+                scatter_dimension=0,
+                tiled=True,
+            )
+        )
+    return jnp.concatenate(pieces, 0)
 
 
 def solution(mesh):

time: 540 us -> 460 us (0.85)
  matrix products: 293 us -> 196 us
  waiting for transfers between devices: 97 us -> 118 us
    dot_general x64 -> x3, matrix products: 116 us -> 11.5 us  [body(): jnp.einsum('hnpi,hnpj->hnij', key_decayed[:, :, step], updated_value_rows...]
    dot_general x11 -> x31, matrix products: 68.4 us -> 109 us  [block_product(): jnp.einsum('hnij,hnjk->hnik', former, latter, precision=exact_matmul_mode)]
    dot_general x39 -> x10, matrix products: 61.7 us -> 22.3 us  [matmul_heads(): jnp.einsum('hij,hjk->hik', former, latter, precision=exact_matmul_mode)]
    reduce_scatter x1 -> x4, waiting for transfers between devices: 89 us -> 109 us  [body(): lax.psum_scatter(jnp.dot(normed, out_weight, preferred_element_type=jnp.f...]
    transpose x2 -> x0, local copies, waits for them, and re-layouts: 10.1 us -> none  [the longest x1 5.61 us: body(): attended = outputs.transpose(0, 2, 1, 3).reshape(tokens, head_count, DV)]
    dot_general x1 -> x4, matrix products: 6.8 us -> 15.5 us  [body(): jnp.dot(normed, out_weight, preferred_element_type=jnp.float32)]
    slice x0 -> x3, local copies, waits for them, and re-layouts: none -> 6.57 us  [the longest x1 4.4 us: body(): fresh_values = solved[..., :DV]]
  transfers between devices with their start and end apart: 9 -> 12, of which waited for: 8 -> 11; matrix products, arithmetic and copies ran while one was open for 1% -> 6% of each run, Pallas kernels for 0% -> 0%
where the time goes in v1:
time: 460 us; the launch traced here: 452 us
  matrix products  196 us (43%)
  waiting for transfers between devices  118 us (26%)
  other arithmetic  45.7 us (10%)
  starting transfers between devices  44.1 us (10%)
  local copies, waits for them, and re-layouts  33 us (7%)
  between operations  14.1 us (3%)
    dot_general x31, matrix products, block_product(): jnp.einsum('hnij,hnjk->hnik', former, latter, precision=exact_matmul_mode)  109 us
    reduce_scatter x4, waiting for transfers between devices, body(): lax.psum_scatter(jnp.dot(normed, out_weight, preferred_element_type=jnp.f...  109 us
    ppermute x8, starting transfers between devices, passed_along(): return lax.ppermute(block, axis, route)  43.8 us
    dot_general x10, matrix products, matmul_heads(): jnp.einsum('hij,hjk->hik', former, latter, precision=exact_matmul_mode)  22.3 us
    dot_general x1, matrix products, body(): jnp.einsum('hnik,hniv->hnkv', key_decayed, fresh_values, precision=exact_...  18.1 us
    dot_general x1, matrix products, body(): jnp.einsum('hnik,hnij->hnkj', key_decayed, wy_weights, precision=exact_ma...  16.1 us
    dot_general x4, matrix products, body(): jnp.dot(normed, out_weight, preferred_element_type=jnp.float32)  15.5 us
    dot_general x3, matrix products, body(): jnp.einsum('hnpi,hnpj->hnij', key_decayed[:, :, step], updated_value_rows...  11.5 us
  transfers between devices with their start and end apart: 12, of which 11 were waited for; matrix products, arithmetic and copies ran while one was open for 6% of the time, Pallas kernels for 0%

profile of v1, /device:TPU:0, one launch (start us, length us, event | category | flops | bytes accessed | tf_op | source)
XLA Modules:
  0.0 452.1 jit_solution(11389155818480050138)
XLA Ops:
  7.3 2.4 collective-permute-start.1
  14.4 2.7 fusion.15
  18.1 2.2 fusion.139
  20.4 3.4 maximum_convert_fusion
  23.8 6.5 %divide_multiply_fusion = f32[1024,2048]{1,0:T(8,128)} fusion(f32[1027,2048]{1,0:T(8,128)S(1)} %maximum_convert_fusion, f32[2048]{0:T(1024)S(1)} %bitcast.309, f32[2048]{0:T(1024)S(1)} %bitcast.308, f32[2048]{0:T(1024)S(1)} %bitcast.307, f32[2048]{0:T(1024)S(1)} %bitcast.306), kind=kLoop, calls=%fused_computation.18 | loop fusion | flops 23068672 | bytes 41975808 | tf_op jit(solution)/shard_map/jit(silu)/mul | solution.py:58
  30.3 10.9 %reshape.142 = f32[1024,4,512]{2,1,0:T(4,128)} reshape(f32[1024,2048]{1,0:T(8,128)} %divide_multiply_fusion) | data formatting | bytes 16777216 | tf_op jit(solution)/shard_map/reshape | solution.py:58
  41.2 4.5 %multiply_reduce_fusion.1 = (f32[1024,4]{1,0:T(8,128)S(1)}, f32[1024,4]{1,0:T(8,128)S(1)}) fusion(f32[1024,4,512]{2,1,0:T(4,128)} %reshape.142), kind=kLoop, calls=%fused_computation.66 | loop fusion | flops 2088960 | bytes 4227072 | tf_op jit(solution)/shard_map/reduce_sum | solution.py:24
  45.8 6.7 %multiply_convert_fusion.1 = (bf16[1024,4,128]{2,1,0:T(4,128)(2,1)}, bf16[1024,4,128]{2,1,0:T(4,128)(2,1)S(1)}) fusion(f32[1024,4,512]{2,1,0:T(4,128)} %reshape.142, f32[1024,4]{1,0:T(8,128)S(1)} %get-tuple-element.89, f32[1024,4]{1,0:T(8,128)S(1)} %get-tuple-element.88), kind=kLoop, calls=%fused_computation.65 | loop fusion | flops 2621440 | bytes 6324224 | tf_op jit(solution)/shard_map/convert_element_type | solution.py:60
  53.0 2.3 add_subtract_fusion
  55.3 4.7 %fusion.143 = f32[8,16,64,64]{3,2,1,0:T(8,128)S(1)} fusion(f32[8,16,64,64]{3,2,1,0:T(8,128)S(1)} %add_subtract_fusion), kind=kOutput, calls=%fused_computation.198 | convolution fusion | flops 402653184 | bytes 4194304 | tf_op jit(solution)/shard_map/hnij,hnjk->hnik/dot_general | solution.py:32
  60.0 6.2 %add_add_fusion = f32[8,16,64,64]{3,2,1,0:T(8,128)S(1)} fusion(f32[8,16,64,64]{3,2,1,0:T(8,128)S(1)} %add_subtract_fusion, f32[8,16,64,64]{3,2,1,0:T(8,128)S(1)} %fusion.143, f32[64,64]{1,0:T(8,128)S(1)} %fusion.134), kind=kOutput, calls=%fused_computation.42 | convolution fusion | flops 404226048 | bytes 6307840 | tf_op jit(solution)/shard_map/hnij,hnjk->hnik/dot_general | solution.py:32
  66.2 4.7 %fusion.144 = f32[8,16,64,64]{3,2,1,0:T(8,128)S(1)} fusion(f32[8,16,64,64]{3,2,1,0:T(8,128)S(1)} %fusion.143), kind=kOutput, calls=%fused_computation.199 | convolution fusion | flops 402653184 | bytes 4194304 | tf_op jit(solution)/shard_map/hnij,hnjk->hnik/dot_general | solution.py:32
  70.8 4.8 %fusion.33 = f32[1024,4,256]{2,1,0:T(4,128)} fusion(f32[1024,4,512]{2,1,0:T(4,128)} %reshape.142), kind=kLoop, calls=%fused_computation.52 | loop fusion | flops 1048576 | bytes 6291456 | tf_op jit(solution)/shard_map/convert_element_type | solution.py:76
  75.7 5.2 %fusion.145 = f32[8,16,64,64]{3,2,1,0:T(8,128)S(1)} fusion(f32[8,16,64,64]{3,2,1,0:T(8,128)S(1)} %fusion.144), kind=kOutput, calls=%fused_computation.200 | convolution fusion | flops 402653184 | bytes 4194304 | tf_op jit(solution)/shard_map/hnij,hnjk->hnik/dot_general | solution.py:32
  80.9 5.7 %convolution_add_fusion.2 = f32[8,16,64,64]{3,2,1,0:T(8,128)S(1)} fusion(f32[8,16,64,64]{3,2,1,0:T(8,128)S(1)} %add_add_fusion, f32[8,16,64,64]{3,2,1,0:T(8,128)S(1)} %fusion.144), kind=kOutput, calls=%fused_computation.47 | convolution fusion | flops 403177472 | bytes 6291456 | tf_op jit(solution)/shard_map/hnij,hnjk->hnik/dot_general | solution.py:32
  86.6 5.3 %fusion.147 = f32[8,16,64,64]{3,2,1,0:T(8,128)S(1)} fusion(f32[8,16,64,64]{3,2,1,0:T(8,128)S(1)} %fusion.145), kind=kOutput, calls=%fused_computation.202 | convolution fusion | flops 402653184 | bytes 4194304 | tf_op jit(solution)/shard_map/hnij,hnjk->hnik/dot_general | solution.py:32
  91.9 5.6 %fusion.146 = f32[8,16,64,64]{3,2,1,0:T(8,128)S(1)} fusion(f32[8,16,64,64]{3,2,1,0:T(8,128)S(1)} %convolution_add_fusion.2, f32[8,16,64,64]{3,2,1,0:T(8,128)S(1)} %fusion.145), kind=kOutput, calls=%fused_computation.201 | convolution fusion | flops 402653184 | bytes 6291456 | tf_op jit(solution)/shard_map/hnij,hnjk->hnik/dot_general | solution.py:32
  97.5 5.9 %fusion.148 = f32[8,16,64,64]{3,2,1,0:T(8,128)} fusion(f32[8,16,64,64]{3,2,1,0:T(8,128)S(1)} %fusion.147), kind=kOutput, calls=%fused_computation.203 | convolution fusion | flops 402653184 | bytes 4194304 | tf_op jit(solution)/shard_map/hnij,hnjk->hnik/dot_general | solution.py:32
  103.5 6.1 %convolution_add_fusion.1 = f32[8,16,64,64]{3,2,1,0:T(8,128)} fusion(f32[8,16,64,64]{3,2,1,0:T(8,128)S(1)} %fusion.147, f32[8,16,64,64]{3,2,1,0:T(8,128)S(1)} %convolution_add_fusion.2, f32[8,16,64,64]{3,2,1,0:T(8,128)S(1)} %fusion.146), kind=kOutput, calls=%fused_computation.45 | convolution fusion | flops 403701760 | bytes 8388608 | tf_op jit(solution)/shard_map/hnij,hnjk->hnik/dot_general | solution.py:32
  109.6 5.5 %reshape.156 = f32[16,64,8,128]{3,2,1,0:T(8,128)} reshape(f32[1024,4,256]{2,1,0:T(4,128)} %fusion.33) | data formatting | bytes 8388608 | tf_op jit(solution)/shard_map/convert_element_type | solution.py:76
  115.1 4.8 %bitcast_multiply_fusion = f32[8,16,64,128]{3,2,1,0:T(8,128)} fusion(f32[16,64,8,128]{3,2,1,0:T(8,128)} %reshape.156, f32[8,16,64]{2,1,0:T(8,128)S(1)} %mul.284), kind=kLoop, calls=%fused_computation.29 | loop fusion | flops 1048576 | bytes 8421376 | tf_op jit(solution)/shard_map/mul | solution.py:94
  121.3 5.9 %fusion.149 = f32[8,16,64,64]{3,2,1,0:T(8,128)} fusion(f32[8,16,64,64]{3,2,1,0:T(8,128)S(1)} %copy-done, f32[8,16,64,64]{3,2,1,0:T(8,128)S(1)} %copy-done.5), kind=kOutput, calls=%fused_computation.204 | convolution fusion | flops 402653184 | bytes 6291456 | tf_op jit(solution)/shard_map/hnij,hnjk->hnik/dot_general | solution.py:32
  127.2 4.5 convert_multiply_fusion.2
  131.7 12.5 %fusion.8 = f32[8,16,64,256]{3,2,1,0:T(8,128)S(1)} fusion(f32[8,16,64,128]{3,2,1,0:T(8,128)} %get-tuple-element.65, f32[8,16,64,128]{3,2,1,0:T(8,128)} %bitcast_multiply_fusion, f32[8,16,64,64]{3,2,1,0:T(8,128)} %convolution_add_fusion.1, f32[8,16,64,64]{3,2,1,0:T(8,128)} %fusion.149), kind=kOutput, calls=%fused_computation.13 | convolution fusion | flops 1613234176 | bytes 20971520 | tf_op jit(solution)/shard_map/hnij,hnjk->hnik/dot_general | solution.py:32
  144.2 18.1 %fusion.61 = f32[8,16,128,128]{3,2,1,0:T(8,128)} fusion(bf16[8,16,64,128]{3,2,1,0:T(8,128)(2,1)} %bitcast.272, f32[8,16,64]{2,1,0:T(8,128)S(1)} %get-tuple-element.68, f32[8,16,64,256]{3,2,1,0:T(8,128)S(1)} %fusion.8), kind=kOutput, calls=%fused_computation.85 | convolution fusion | flops 1612709888 | bytes 14745600 | tf_op jit(solution)/shard_map/hnik,hniv->hnkv/dot_general | solution.py:113
  162.4 4.4 fusion.138
  166.8 16.1 %multiply_subtract_fusion = f32[8,16,128,128]{3,2,1,0:T(8,128)S(1)} fusion(f32[128,128]{1,0:T(8,128)S(1)} %fusion.133, f32[8,16]{1,0:T(8,128)S(1)} %bitcast_exponential_fusion, bf16[8,16,64,128]{3,2,1,0:T(8,128)(2,1)S(1)} %bitcast.273, f32[8,16,64]{2,1,0:T(8,128)S(1)} %get-tuple-element.68, f32[8,16,64,256]{3,2,1,0:T(8,128)S(1)} %fusion.8), kind=kOutput, calls=%fused_computation.17 | convolution fusion | flops 1616904192 | bytes 14815232 | tf_op jit(solution)/shard_map/hnik,hnij->hnkj/dot_general | solution.py:110
  182.9 4.7 %fusion.18 = f32[8,8,128,128]{3,2,1,0:T(8,128)S(1)} fusion(f32[8,16,128,128]{3,2,1,0:T(8,128)S(1)} %multiply_subtract_fusion), kind=kOutput, calls=%fused_computation.33 | convolution fusion | flops 1610612736 | bytes 12582912 | tf_op jit(solution)/shard_map/hnij,hnjk->hnik/dot_general | solution.py:32
  187.6 6.1 %slice_add_fusion = f32[8,8,128,128]{3,2,1,0:T(8,128)} fusion(f32[8,16,128,128]{3,2,1,0:T(8,128)S(1)} %copy-done.4, f32[8,16,128,128]{3,2,1,0:T(8,128)S(1)} %multiply_subtract_fusion), kind=kOutput, calls=%fused_computation.30 | convolution fusion | flops 1611661312 | bytes 16777216 | tf_op jit(solution)/shard_map/hnij,hnjk->hnik/dot_general | solution.py:32
  193.7 2.2 fusion.36
  195.9 2.2 slice_add_fusion.1
  202.5 68.3 %while.11 = (s32[]{:T(128)}, f32[8,128,128]{2,1,0:T(8,128)S(1)}, f32[8,128,128]{2,1,0:T(8,128)S(1)}, f32[8,128,128]{2,1,0:T(8,128)}, s32[]{:T(128)}, /*index=5*/s32[]{:T(128)}) while((s32[]{:T(128)}, f32[8,128,128]{2,1,0:T(8,128)S(1)}, f32[8,128,128]{2,1,0:T(8,128)S(1)}, f32[8,128,128]{2,1,0:T(8,128)}, s32[]{:T(128)}, ...), condition=%wide.region_4.5_spmd.clone, body=%wide.region_3.4_spmd.clone.sunk | while | flops 201850880 | bytes 3670135 | solution.py:145
  202.5 2.4 fusion.189
  204.9 4.5 collective-permute-start
  210.9 2.4 fusion.189
  213.3 4.2 collective-permute-start
  218.9 2.4 fusion.189
  221.3 6.5 %collective-permute-start = (bf16[8,128,128]{2,1,0:T(8,128)(2,1)}, bf16[8,128,128]{2,1,0:T(8,128)(2,1)S(1)}, u32[]{:S(2)}, u32[]{:S(2)}) collective-permute-start(bf16[8,128,128]{2,1,0:T(8,128)(2,1)} %fusion.189), channel_id=1, source_target_pairs={{0,4},{4,8},{8,12},{12,16},{16,20},{20,24},{24,28},{1,5},{5,9},{9,... | collective-permute-start | bytes 786440 | tf_op jit(solution)/shard_map/while/body/eval_jaxpr/ppermute | solution.py:20
  229.2 2.4 fusion.189
  231.6 6.5 %collective-permute-start = (bf16[8,128,128]{2,1,0:T(8,128)(2,1)}, bf16[8,128,128]{2,1,0:T(8,128)(2,1)S(1)}, u32[]{:S(2)}, u32[]{:S(2)}) collective-permute-start(bf16[8,128,128]{2,1,0:T(8,128)(2,1)} %fusion.189), channel_id=1, source_target_pairs={{0,4},{4,8},{8,12},{12,16},{16,20},{20,24},{24,28},{1,5},{5,9},{9,... | collective-permute-start | bytes 786440 | tf_op jit(solution)/shard_map/while/body/eval_jaxpr/ppermute | solution.py:20
  239.6 2.4 fusion.189
  242.0 6.5 %collective-permute-start = (bf16[8,128,128]{2,1,0:T(8,128)(2,1)}, bf16[8,128,128]{2,1,0:T(8,128)(2,1)S(1)}, u32[]{:S(2)}, u32[]{:S(2)}) collective-permute-start(bf16[8,128,128]{2,1,0:T(8,128)(2,1)} %fusion.189), channel_id=1, source_target_pairs={{0,4},{4,8},{8,12},{12,16},{16,20},{20,24},{24,28},{1,5},{5,9},{9,... | collective-permute-start | bytes 786440 | tf_op jit(solution)/shard_map/while/body/eval_jaxpr/ppermute | solution.py:20
  249.9 2.4 fusion.189
  252.4 6.5 %collective-permute-start = (bf16[8,128,128]{2,1,0:T(8,128)(2,1)}, bf16[8,128,128]{2,1,0:T(8,128)(2,1)S(1)}, u32[]{:S(2)}, u32[]{:S(2)}) collective-permute-start(bf16[8,128,128]{2,1,0:T(8,128)(2,1)} %fusion.189), channel_id=1, source_target_pairs={{0,4},{4,8},{8,12},{12,16},{16,20},{20,24},{24,28},{1,5},{5,9},{9,... | collective-permute-start | bytes 786440 | tf_op jit(solution)/shard_map/while/body/eval_jaxpr/ppermute | solution.py:20
  260.3 2.4 fusion.189
  262.7 6.5 %collective-permute-start = (bf16[8,128,128]{2,1,0:T(8,128)(2,1)}, bf16[8,128,128]{2,1,0:T(8,128)(2,1)S(1)}, u32[]{:S(2)}, u32[]{:S(2)}) collective-permute-start(bf16[8,128,128]{2,1,0:T(8,128)(2,1)} %fusion.189), channel_id=1, source_target_pairs={{0,4},{4,8},{8,12},{12,16},{16,20},{20,24},{24,28},{1,5},{5,9},{9,... | collective-permute-start | bytes 786440 | tf_op jit(solution)/shard_map/while/body/eval_jaxpr/ppermute | solution.py:20
  280.0 3.7 multiply_add_fusion.2
  290.3 3.7 multiply_add_fusion.1
  294.0 2.1 fusion.86
  297.3 4.0 multiply_add_fusion
  301.3 2.1 fusion.95
  305.9 2.2 multiply_reduce_fusion.2
  308.2 2.2 multiply_reduce_fusion.3
  310.5 2.1 multiply_reduce_fusion.4
  312.6 2.1 multiply_reduce_fusion.5
  317.1 2.2 convolution_convert_fusion
  319.9 4.4 convolution_convert_fusion.3
  324.8 4.4 convolution_convert_fusion.2
  329.6 4.4 convolution_convert_fusion.1
  334.1 24.5 %reduce-scatter.11.cloned.1.call-done = bf16[64,2048]{1,0:T(8,128)(2,1)} async-done(((bf16[256,2048]{1,0:T(8,128)(2,1)}), bf16[64,2048]{1,0:T(8,128)(2,1)}) %reduce-scatter.11.cloned.1.call-update) | async-done | bytes 262160 | tf_op jit(solution)/shard_map/reduce_scatter | solution.py:188
  358.6 28.2 %reduce-scatter.5.cloned.1.call-done = bf16[64,2048]{1,0:T(8,128)(2,1)} async-done(((bf16[256,2048]{1,0:T(8,128)(2,1)}), bf16[64,2048]{1,0:T(8,128)(2,1)}) %reduce-scatter.5.cloned.1.call-update) | async-done | bytes 262160 | tf_op jit(solution)/shard_map/reduce_scatter | solution.py:188
  386.8 28.1 %reduce-scatter.7.cloned.1.call-done = bf16[64,2048]{1,0:T(8,128)(2,1)} async-done(((bf16[256,2048]{1,0:T(8,128)(2,1)}), bf16[64,2048]{1,0:T(8,128)(2,1)}) %reduce-scatter.7.cloned.1.call-update) | async-done | bytes 262160 | tf_op jit(solution)/shard_map/reduce_scatter | solution.py:188
  415.0 28.1 %reduce-scatter.9.cloned.1.call-done = bf16[64,2048]{1,0:T(8,128)(2,1)} async-done(((bf16[256,2048]{1,0:T(8,128)(2,1)}), bf16[64,2048]{1,0:T(8,128)(2,1)}) %reduce-scatter.9.cloned.1.call-update) | async-done | bytes 262160 | tf_op jit(solution)/shard_map/reduce_scatter | solution.py:188
  443.1 2.3 pad_maximum_fusion.1
  (110 shorter events, 45.5 us)
Async XLA Ops:
  6.5 352.1 %reduce-scatter.11.cloned.1.call-start = ((), (), s32[]{:S(2)}) async-start(), calls=%async_computation.7 | async-start | bytes 1310720 | tf_op jit(solution)/shard_map/reduce_scatter | solution.py:188
  7.3 13.0 %collective-permute-start.1 = (bf16[3,2048]{1,0:T(4,128)(2,1)S(1)}, bf16[3,2048]{1,0:T(4,128)(2,1)S(1)}, u32[]{:S(2)}, u32[]{:S(2)}) collective-permute-start(bf16[3,2048]{1,0:T(4,128)(2,1)S(1)} %slice.195), channel_id=1, source_target_pairs={{0,4},{4,8},{8,12},{12,16},{16,20},{20,24},{24,28},{1,5},{5,9},{9,... | collective-permute-start | bytes 36872 | tf_op jit(solution)/shard_map/ppermute | solution.py:20
  20.3 32.7 %copy-start.16 = (pred[64,64]{1,0:T(8,128)(4,1)}, pred[64,64]{1,0:T(8,128)(4,1)S(1)}, u32[]{:S(2)}) copy-start(pred[64,64]{1,0:T(8,128)(4,1)S(1)} %get-tuple-element.90) | copy-start | bytes 12292
  53.0 74.2 %copy-start.1 = (bf16[1024,4,2,128]{3,0,2,1:T(8,128)(2,1)}, bf16[1024,4,2,128]{3,0,2,1:T(8,128)(2,1)S(1)}, u32[]{:S(2)}) copy-start(bf16[1024,4,2,128]{3,0,2,1:T(8,128)(2,1)S(1)} %broadcast_in_dim.24) | copy-start | bytes 6291460
  115.1 4.8 %copy-start = (f32[8,16,64,64]{3,2,1,0:T(8,128)S(1)}, f32[8,16,64,64]{3,2,1,0:T(8,128)}, u32[]{:S(2)}) copy-start(f32[8,16,64,64]{3,2,1,0:T(8,128)} %convolution_add_fusion.1) | copy-start | bytes 6291460
  115.1 6.2 %copy-start.5 = (f32[8,16,64,64]{3,2,1,0:T(8,128)S(1)}, f32[8,16,64,64]{3,2,1,0:T(8,128)}, u32[]{:S(2)}) copy-start(f32[8,16,64,64]{3,2,1,0:T(8,128)} %fusion.148) | copy-start | bytes 6291460
  162.4 4.4 copy-start.2
  182.9 4.7 %copy-start.4 = (f32[8,16,128,128]{3,2,1,0:T(8,128)S(1)}, f32[8,16,128,128]{3,2,1,0:T(8,128)}, u32[]{:S(2)}) copy-start(f32[8,16,128,128]{3,2,1,0:T(8,128)} %fusion.61) | copy-start | bytes 25165828
  193.7 2.2 copy-start.10
  198.1 4.4 copy-start.9
  204.9 5.9 %collective-permute-start = (bf16[8,128,128]{2,1,0:T(8,128)(2,1)}, bf16[8,128,128]{2,1,0:T(8,128)(2,1)S(1)}, u32[]{:S(2)}, u32[]{:S(2)}) collective-permute-start(bf16[8,128,128]{2,1,0:T(8,128)(2,1)} %fusion.189), channel_id=1, source_target_pairs={{0,4},{4,8},{8,12},{12,16},{16,20},{20,24},{24,28},{1,5},{5,9},{9,... | collective-permute-start | bytes 786440 | tf_op jit(solution)/shard_map/while/body/eval_jaxpr/ppermute | solution.py:20
  213.3 5.5 %collective-permute-start = (bf16[8,128,128]{2,1,0:T(8,128)(2,1)}, bf16[8,128,128]{2,1,0:T(8,128)(2,1)S(1)}, u32[]{:S(2)}, u32[]{:S(2)}) collective-permute-start(bf16[8,128,128]{2,1,0:T(8,128)(2,1)} %fusion.189), channel_id=1, source_target_pairs={{0,4},{4,8},{8,12},{12,16},{16,20},{20,24},{24,28},{1,5},{5,9},{9,... | collective-permute-start | bytes 786440 | tf_op jit(solution)/shard_map/while/body/eval_jaxpr/ppermute | solution.py:20
  221.3 7.9 %collective-permute-start = (bf16[8,128,128]{2,1,0:T(8,128)(2,1)}, bf16[8,128,128]{2,1,0:T(8,128)(2,1)S(1)}, u32[]{:S(2)}, u32[]{:S(2)}) collective-permute-start(bf16[8,128,128]{2,1,0:T(8,128)(2,1)} %fusion.189), channel_id=1, source_target_pairs={{0,4},{4,8},{8,12},{12,16},{16,20},{20,24},{24,28},{1,5},{5,9},{9,... | collective-permute-start | bytes 786440 | tf_op jit(solution)/shard_map/while/body/eval_jaxpr/ppermute | solution.py:20
  231.6 7.9 %collective-permute-start = (bf16[8,128,128]{2,1,0:T(8,128)(2,1)}, bf16[8,128,128]{2,1,0:T(8,128)(2,1)S(1)}, u32[]{:S(2)}, u32[]{:S(2)}) collective-permute-start(bf16[8,128,128]{2,1,0:T(8,128)(2,1)} %fusion.189), channel_id=1, source_target_pairs={{0,4},{4,8},{8,12},{12,16},{16,20},{20,24},{24,28},{1,5},{5,9},{9,... | collective-permute-start | bytes 786440 | tf_op jit(solution)/shard_map/while/body/eval_jaxpr/ppermute | solution.py:20
  242.0 7.9 %collective-permute-start = (bf16[8,128,128]{2,1,0:T(8,128)(2,1)}, bf16[8,128,128]{2,1,0:T(8,128)(2,1)S(1)}, u32[]{:S(2)}, u32[]{:S(2)}) collective-permute-start(bf16[8,128,128]{2,1,0:T(8,128)(2,1)} %fusion.189), channel_id=1, source_target_pairs={{0,4},{4,8},{8,12},{12,16},{16,20},{20,24},{24,28},{1,5},{5,9},{9,... | collective-permute-start | bytes 786440 | tf_op jit(solution)/shard_map/while/body/eval_jaxpr/ppermute | solution.py:20
  252.4 7.9 %collective-permute-start = (bf16[8,128,128]{2,1,0:T(8,128)(2,1)}, bf16[8,128,128]{2,1,0:T(8,128)(2,1)S(1)}, u32[]{:S(2)}, u32[]{:S(2)}) collective-permute-start(bf16[8,128,128]{2,1,0:T(8,128)(2,1)} %fusion.189), channel_id=1, source_target_pairs={{0,4},{4,8},{8,12},{12,16},{16,20},{20,24},{24,28},{1,5},{5,9},{9,... | collective-permute-start | bytes 786440 | tf_op jit(solution)/shard_map/while/body/eval_jaxpr/ppermute | solution.py:20
  262.7 7.9 %collective-permute-start = (bf16[8,128,128]{2,1,0:T(8,128)(2,1)}, bf16[8,128,128]{2,1,0:T(8,128)(2,1)S(1)}, u32[]{:S(2)}, u32[]{:S(2)}) collective-permute-start(bf16[8,128,128]{2,1,0:T(8,128)(2,1)} %fusion.189), channel_id=1, source_target_pairs={{0,4},{4,8},{8,12},{12,16},{16,20},{20,24},{24,28},{1,5},{5,9},{9,... | collective-permute-start | bytes 786440 | tf_op jit(solution)/shard_map/while/body/eval_jaxpr/ppermute | solution.py:20
  270.8 5.4 %copy-start.8 = (f32[8,16,64,128]{3,2,1,0:T(8,128)S(1)}, f32[8,16,64,128]{3,2,1,0:T(8,128)}, u32[]{:S(2)}) copy-start(f32[8,16,64,128]{3,2,1,0:T(8,128)} %get-tuple-element.64) | copy-start | bytes 12582916
  274.4 2.3 copy-start.6
  274.4 3.6 copy-start.7
  283.8 2.0 copy-start.11
  283.8 2.5 copy-start.3
  283.8 2.5 copy-start.17
  310.4 4.4 copy-start.12
  310.4 4.3 copy-start.13
  310.4 4.3 copy-start.14
  310.4 4.3 copy-start.15
  310.4 4.3 copy-start.18
  314.8 2.3 copy-start.19
  319.3 67.5 %reduce-scatter.5.cloned.1.call-start = ((), (), s32[]{:S(2)}) async-start(), calls=%async_computation.4 | async-start | bytes 1310720 | tf_op jit(solution)/shard_map/reduce_scatter | solution.py:188
  324.4 90.6 %reduce-scatter.7.cloned.1.call-start = ((), (), s32[]{:S(2)}) async-start(), calls=%async_computation.5 | async-start | bytes 1310720 | tf_op jit(solution)/shard_map/reduce_scatter | solution.py:188
  329.2 113.8 %reduce-scatter.9.cloned.1.call-start = ((), (), s32[]{:S(2)}) async-start(), calls=%async_computation.6 | async-start | bytes 1310720 | tf_op jit(solution)/shard_map/reduce_scatter | solution.py:188
Sparse Core Ops, SparseCore 0:
  319.4 39.1 reduce-scatter.10
  361.0 25.7 reduce-scatter.4
  389.1 25.7 reduce-scatter.6
  417.2 25.7 reduce-scatter.8
